TPU v7x, 256 devices: a whole 4x4x8 slice. The times are simulated.
256 devices in a mesh: req: 32 (over y, z), tp: 8 (over x, core).
Axes of the slice: x: 4, y: 4, z: 8, core: 2. Of those that a mesh axis runs over, the one named last changes fastest.
Arguments:
- tokens: bfloat16 [32768, 1792], P(('req', 'tp')), may hold values from -6 to 6
- norm_gain: float32 [1792], replicated, may hold values from 0.25 to 1.75
- ffn_gain: float32 [1792], replicated, may hold values from 0.25 to 1.75
- mix_weight: bfloat16 [1792, 4, 1792], P('req', None, 'tp'), may hold values from -0.125 to 0.125
- out_weight: bfloat16 [1792, 1792], P('tp', 'req'), may hold values from -0.125 to 0.125
- ffn_weight: bfloat16 [1792, 2, 7168], P('req', None, 'tp'), may hold values from -0.125 to 0.125
- down_weight: bfloat16 [7168, 1792], P('tp', 'req'), may hold values from -0.0625 to 0.0625
- conv_taps: float32 [3, 1792], P(None, 'tp'), may hold values from -3 to 3
- past_cache: bfloat16 [32, 2, 64, 1792], P('req', None, None, 'tp'), may hold values from -210 to 210
- cached_len: int32 [32], P('req'), may hold values from 0 to 8192, as said below
Outputs:
- layer_out: bfloat16 [32768, 1792], P(('req', 'tp'))
- new_cache: bfloat16 [32, 2, 64, 1792], P('req', None, None, 'tp')
Inputs may be any that keep to these rules, and one draw needn't show every extreme that they name: `cached_len`: one request has exactly 8192 cached positions and another fewer than 64.
All inputs are finite; a program needn't handle non-finite values.
Results may differ from a plain program's by a relative error of at most 0.02.
Values may be sent and summed in bfloat16 or wider, within the bound.
No kernel may reach another device: no remote copies, remote signals or barrier semaphores. Data moves between devices by JAX's collectives and lax.ppermute only.
A program may use at most 64 MiB of HBM per device.

v0:
```python
import math
import jax
import jax.numpy as jnp
from jax import lax
from jax.sharding import PartitionSpec as P

HD = 112
WIN = 64


def normed(row_vals, gain):
    floats = row_vals.astype(jnp.float32)
    scaled = floats * lax.rsqrt(jnp.mean(floats * floats, axis=-1, keepdims=True) + 1e-05)
    return (scaled * gain).astype(jnp.bfloat16)


def window_attend(queries, key_rows, value_rows, length, window):
    row_count, head_count, head_size = queries.shape
    nb = row_count // window
    score_scale = 1.0 / math.sqrt(head_size)
    qb = queries.reshape(nb, window, head_count, head_size)

    def blocks(rows):
        lo = rows[:row_count].reshape(nb, window, head_count, head_size)
        hi = rows[window:].reshape(nb, window, head_count, head_size)
        return jnp.concatenate([lo, hi], axis=1)

    kb = blocks(key_rows)
    vb = blocks(value_rows)
    scores = jnp.einsum("bqhd,bkhd->bhqk", qb, kb, preferred_element_type=jnp.float32) * score_scale
    i = jnp.arange(window, dtype=jnp.int32)[:, None]
    j = jnp.arange(2 * window, dtype=jnp.int32)[None, :]
    b = jnp.arange(nb, dtype=jnp.int32)[:, None, None]
    usable = (j > i)[None] & (j <= i + window)[None] & (b * window + j >= window - length)
    scores = jnp.where(usable[:, None], scores, -1e30)
    row_max = jnp.max(scores, axis=-1, keepdims=True)
    exponent = jnp.exp(scores - row_max)
    weights = (exponent / jnp.sum(exponent, axis=-1, keepdims=True)).astype(jnp.bfloat16)
    out = jnp.einsum("bhqk,bkhd->bqhd", weights, vb, preferred_element_type=jnp.float32)
    return out.reshape(row_count, head_count, head_size)


def mix_request(projected, cache_rows, length, tap_table, window, head_size):
    row_count, feat_width = (projected.shape[0], projected.shape[2])
    time_order = (length + jnp.arange(window, dtype=jnp.int32)) % window
    earlier = cache_rows[:, time_order]
    key_rows = jnp.concatenate([earlier[0], projected[:, 1]], axis=0)
    value_rows = jnp.concatenate([earlier[1], projected[:, 2]], axis=0)
    head_count = feat_width // head_size
    attended = window_attend(
        projected[:, 0].reshape(row_count, head_count, head_size),
        key_rows.reshape(-1, head_count, head_size),
        value_rows.reshape(-1, head_count, head_size),
        length,
        window,
    ).reshape(row_count, feat_width)
    positions = jnp.arange(window + row_count, dtype=jnp.int32)
    alive_mask = (positions >= window - length)[:, None]
    masked_values = jnp.where(alive_mask, value_rows.astype(jnp.float32), jnp.float32(0.0))
    tap_count = tap_table.shape[0]
    convolved = jnp.zeros((row_count, feat_width), jnp.float32)
    for tap_index in range(tap_count):
        begin_row = window - (tap_count - 1) + tap_index
        convolved = (
            convolved + tap_table[tap_index] * masked_values[begin_row : begin_row + row_count]
        )
    mixed_heads = (attended + projected[:, 3].astype(jnp.float32) * convolved).astype(jnp.bfloat16)
    slot_source = (
        row_count - window + (jnp.arange(window, dtype=jnp.int32) - length - row_count) % window
    )
    renewed = jnp.stack([projected[:, 1], projected[:, 2]])[:, slot_source]
    return (mixed_heads, renewed)


def gather_packed(pieces):
    widths = [p.shape[1] for p in pieces]
    got = lax.all_gather(jnp.concatenate(pieces, axis=1), "req", axis=0, tiled=True)
    parts = []
    start = 0
    for w in widths:
        parts.append(got[:, start : start + w])
        start += w
    return parts


def core_swap(x):
    return lax.ppermute(x, "tpc", [(0, 1), (1, 0)])


def mlp_rows(rows, ffn_all, down_t, ffn_width):
    gate_up = jnp.dot(rows, ffn_all, preferred_element_type=jnp.float32)
    activated = (jax.nn.silu(gate_up[:, :ffn_width]) * gate_up[:, ffn_width:]).astype(jnp.bfloat16)
    out = lax.dot_general(
        activated, down_t, (((1,), (1,)), ((), ())), preferred_element_type=jnp.float32
    )
    return out.astype(jnp.bfloat16)


def local(
    tokens,
    norm_gain,
    ffn_gain,
    mix_weight,
    out_weight,
    ffn_weight,
    down_weight,
    conv_taps,
    past_cache,
    cached_len,
):
    feat_width = mix_weight.shape[2]
    ffn_width = ffn_weight.shape[2]
    rows = mix_weight.shape[0]
    mix_all, out_t = gather_packed([mix_weight.reshape(rows, -1), out_weight.T])
    ffn_all, down_t = gather_packed([ffn_weight.reshape(rows, -1), down_weight.T])
    nxt = lax.axis_size("tpx")
    tok_mine = lax.all_to_all(
        jnp.tile(normed(tokens, norm_gain)[None], (nxt, 1, 1)), "tpx", 0, 0, tiled=True
    )
    tok_theirs = core_swap(tok_mine)
    first = lax.axis_index("tpc") == 0
    pairs = jnp.stack(
        [jnp.where(first, tok_mine, tok_theirs), jnp.where(first, tok_theirs, tok_mine)], axis=1
    )
    normed_all = pairs.reshape((-1,) + tok_mine.shape[2:])
    row_total = normed_all.shape[0]
    projected = jnp.dot(normed_all, mix_all, preferred_element_type=jnp.float32)
    projected = projected.astype(jnp.bfloat16).reshape(row_total, 4, feat_width)
    mixed_heads, renewed = mix_request(projected, past_cache[0], cached_len[0], conv_taps, WIN, HD)
    nx = lax.axis_size("tpx")
    nc = lax.axis_size("tpc")
    me_c = lax.axis_index("tpc")
    by_core = mixed_heads.reshape(nx, nc, -1, feat_width)
    mine_rows = lax.dynamic_index_in_dim(by_core, me_c, axis=1, keepdims=False)
    their_rows = lax.dynamic_index_in_dim(by_core, 1 - me_c, axis=1, keepdims=False)

    def out_rows(r):
        return lax.dot_general(
            r.reshape(-1, feat_width),
            out_t,
            (((1,), (1,)), ((), ())),
            preferred_element_type=jnp.float32,
        ).astype(jnp.bfloat16)

    back = core_swap(out_rows(their_rows))
    pair = (out_rows(mine_rows).astype(jnp.float32) + back.astype(jnp.float32)).astype(jnp.bfloat16)
    chips = lax.all_to_all(pair.reshape((nx, -1) + pair.shape[1:]), "tpx", 0, 0, tiled=True)
    attn_part = chips.astype(jnp.float32).sum(axis=0)
    residual = (tokens.astype(jnp.float32) + attn_part).astype(jnp.bfloat16)
    nx = lax.axis_size("tpx")
    mine = lax.all_to_all(
        jnp.tile(normed(residual, ffn_gain)[None], (nx, 1, 1)), "tpx", 0, 0, tiled=True
    )
    flat = mine.reshape((-1,) + mine.shape[2:])
    theirs = core_swap(flat)
    part_mine = mlp_rows(flat, ffn_all, down_t, ffn_width)
    part_theirs = mlp_rows(theirs, ffn_all, down_t, ffn_width)
    back = core_swap(part_theirs)
    pair = (part_mine.astype(jnp.float32) + back.astype(jnp.float32)).astype(jnp.bfloat16)
    cols = pair.shape[1] // 2
    on_sc = lax.psum_scatter(pair[:, :cols], "tpx", scatter_dimension=0, tiled=True)
    by_a2a = lax.all_to_all(pair[:, cols:].reshape((nx, -1, cols)), "tpx", 0, 0, tiled=True)
    ffn_part = jnp.concatenate(
        [on_sc.astype(jnp.float32), by_a2a.astype(jnp.float32).sum(axis=0)], axis=1
    )
    layer_out = (residual.astype(jnp.float32) + ffn_part).astype(jnp.bfloat16)
    return (layer_out, renewed[None])


def solution(mesh):
    n_req, n_tp = mesh.devices.shape
    split = jax.sharding.Mesh(mesh.devices.reshape(n_req, n_tp // 2, 2), ("req", "tpx", "tpc"))
    tp = ("tpx", "tpc")
    in_specs = (
        P(("req",) + tp, None),
        P(),
        P(),
        P("req", None, tp),
        P(tp, "req"),
        P("req", None, tp),
        P(tp, "req"),
        P(None, tp),
        P("req", None, None, tp),
        P("req"),
    )
    out_specs = (P(("req",) + tp, None), P("req", None, None, tp))
    return jax.shard_map(local, mesh=split, in_specs=in_specs, out_specs=out_specs, check_vma=False)
```

profile of v0, /device:TPU:1, one launch (start us, length us, event | category | flops | bytes accessed | tf_op | source)
XLA Modules:
  0.0 253.3 jit_solution(17294180878208792725)
XLA Ops:
  8.3 1.4 pad_maximum_fusion.5
  10.8 1.6 pad_maximum_fusion.4
  13.0 27.3 %all_to_all.20 = bf16[4,128,1792]{2,1,0:T(8,128)(2,1)S(1)} all-to-all(bf16[4,128,1792]{2,1,0:T(8,128)(2,1)S(1)} %tile.4), channel_id=1, replica_groups=mesh['req'=32,'tpx'=4,'tpc'=2] {'tpx'}, dimensions={0} | all-to-all | bytes 3670016 | tf_op jit(solution)/shard_map/all_to_all | solution.py:117
  40.3 2.0 collective-permute-start
  45.8 1.7 select_bitcast_fusion.1
  47.6 2.1 pad_maximum_fusion
  49.6 44.5 %all-gather.3.cloned.1.call-done = bf16[1792,1120]{1,0:T(8,128)(2,1)} async-done(((bf16[56,1120]{1,0:T(8,128)(2,1)}), bf16[1792,1120]{1,0:T(8,128)(2,1)}) %all-gather.3.cloned.1.call-update) | async-done | bytes 4014096 | tf_op jit(solution)/shard_map/all_gather | solution.py:77
  94.1 6.6 %fusion.13 = bf16[1024,896]{0,1:T(8,128)(2,1)S(1)} fusion(bf16[1024,1792]{1,0:T(8,128)(2,1)} %bitcast.68, bf16[1792,1120]{1,0:T(8,128)(2,1)} %all-gather.3.cloned.1.call-done), kind=kOutput, calls=%fused_computation.26 | convolution fusion | flops 3289251840 | bytes 8716288 | tf_op jit(solution)/shard_map/dot_general | solution.py:127
  103.9 2.6 %reshape.295 = bf16[16,64,2,112]{1,0,3,2:T(8,128)(2,1)} reshape(bf16[1024,1,224]{0,2,1:T(8,128)(2,1)} %get-tuple-element.14) | data formatting | bytes 917504 | tf_op jit(solution)/shard_map/reshape;reshape;squeeze | solution.py:21
  109.7 2.2 reshape.267
  111.9 2.1 copy.32
  114.1 2.1 copy.33
  116.2 2.4 fusion.69
  118.7 3.0 %fusion.18 = f32[16,2,64,128]{3,2,1,0:T(8,128)} fusion(bf16[16,64,2,112]{1,3,2,0:T(8,128)(2,1)S(1)} %copy.39, bf16[16,64,2,112]{1,3,2,0:T(8,128)(2,1)S(1)} %copy.38, bf16[16,64,2,112]{1,0,3,2:T(8,128)(2,1)} %reshape.295, pred[16,64,128]{2,1,0:T(8,128)(4,1)S(1)} %broadcast_and_fusion), kind=kOutput, calls=%fused_computation.36 | convolution fusion | flops 61079552 | bytes 2555904 | tf_op jit(solution)/shard_map/bqhd,bkhd->bhqk/dot_general | solution.py:30
  121.7 6.3 %convolution_bitcast_fusion = f32[16,64,2,112]{3,1,2,0:T(8,128)S(1)} fusion(bf16[16,64,2,112]{1,3,2,0:T(8,128)(2,1)} %copy.33, bf16[16,64,2,112]{1,3,2,0:T(8,128)(2,1)} %copy.32, f32[16,2,64]{2,1,0:T(2,128)S(1)} %fusion.69, f32[16,2,64,128]{3,2,1,0:T(8,128)} %fusion.18), kind=kOutput, calls=%fused_computation.37 | convolution fusion | flops 61343872 | bytes 2891776 | tf_op jit(solution)/shard_map/bhqk,bkhd->bqhd/dot_general | solution.py:39
  131.1 1.9 convolution_convert_fusion
  133.0 3.3 %collective-permute-start.1 = (bf16[512,1792]{1,0:T(8,128)(2,1)S(1)}, bf16[512,1792]{1,0:T(8,128)(2,1)S(1)}, u32[]{:S(2)}, u32[]{:S(2)}) collective-permute-start(bf16[512,1792]{1,0:T(8,128)(2,1)S(1)} %convolution_convert_fusion), channel_id=1, source_target_pairs={{0,1},{1,0},{2,3},{3,2},{4,5},{5,4},{6,7},{7,6},{8,9},{9,8},{10,11... | collective-permute-start | bytes 5505032 | tf_op jit(solution)/shard_map/ppermute | solution.py:87
  136.3 3.4 %collective-permute-done.1 = bf16[512,1792]{1,0:T(8,128)(2,1)S(1)} collective-permute-done((bf16[512,1792]{1,0:T(8,128)(2,1)S(1)}, bf16[512,1792]{1,0:T(8,128)(2,1)S(1)}, u32[]{:S(2)}, u32[]{:S(2)}) %collective-permute-start.1) | collective-permute-done | bytes 1835040 | tf_op jit(solution)/shard_map/ppermute | solution.py:87
  139.7 1.9 add_convert_fusion.1
  141.6 26.5 %all_to_all.21 = bf16[4,128,1792]{2,1,0:T(8,128)(2,1)S(1)} all-to-all(bf16[4,128,1792]{2,1,0:T(8,128)(2,1)S(1)} %bitcast.67), channel_id=1, replica_groups=mesh['req'=32,'tpx'=4,'tpc'=2] {'tpx'}, dimensions={0} | all-to-all | bytes 3670016 | tf_op jit(solution)/shard_map/all_to_all | solution.py:147
  169.1 24.2 %all_to_all.22 = bf16[4,128,1792]{2,1,0:T(8,128)(2,1)S(1)} all-to-all(bf16[4,128,1792]{2,1,0:T(8,128)(2,1)S(1)} %tile.5), channel_id=1, replica_groups=mesh['req'=32,'tpx'=4,'tpc'=2] {'tpx'}, dimensions={0} | all-to-all | bytes 3670016 | tf_op jit(solution)/shard_map/all_to_all | solution.py:151
  193.3 2.7 %collective-permute-start.2 = (bf16[512,1792]{1,0:T(8,128)(2,1)S(1)}, bf16[512,1792]{1,0:T(8,128)(2,1)}, u32[]{:S(2)}, u32[]{:S(2)}) collective-permute-start(bf16[512,1792]{1,0:T(8,128)(2,1)S(1)} %bitcast.70), channel_id=1, source_target_pairs={{0,1},{1,0},{2,3},{3,2},{4,5},{5,4},{6,7},{7,6},{8,9},{9,8},{10,11... | collective-permute-start | bytes 5505032 | tf_op jit(solution)/shard_map/ppermute | solution.py:87
  196.0 3.5 %collective-permute-done.2 = bf16[512,1792]{1,0:T(8,128)(2,1)} collective-permute-done((bf16[512,1792]{1,0:T(8,128)(2,1)S(1)}, bf16[512,1792]{1,0:T(8,128)(2,1)}, u32[]{:S(2)}, u32[]{:S(2)}) %collective-permute-start.2) | collective-permute-done | bytes 1835040 | tf_op jit(solution)/shard_map/ppermute | solution.py:87
  200.7 7.0 %fusion.1 = f32[512,1792]{1,0:T(8,128)S(1)} fusion(bf16[512,1792]{1,0:T(8,128)(2,1)} %collective-permute-done.2, bf16[1792,2688]{1,0:T(8,128)(2,1)} %all-gather.5.cloned.1.call-done), kind=kOutput, calls=%fused_computation.3 | convolution fusion | flops 3288334336 | bytes 11927552 | tf_op jit(solution)/shard_map/dot_general | solution.py:91
  207.8 2.3 convolution_convert_fusion.2
  211.3 3.5 %fusion.3 = f32[512,1792]{1,0:T(8,128)S(1)} fusion(bf16[512,1792]{1,0:T(8,128)(2,1)S(1)} %bitcast.71, bf16[1792,2688]{1,0:T(8,128)(2,1)S(1)} %copy-done.9), kind=kOutput, calls=%fused_computation.5 | convolution fusion | flops 3288334336 | bytes 11927552 | tf_op jit(solution)/shard_map/dot_general | solution.py:91
  214.8 2.3 add_convert_fusion
  217.1 1.4 fusion.66
  218.6 4.6 %all-to-all-start.3 = ((bf16[4,128,896]{2,1,0:T(8,128)(2,1)}), bf16[4,128,896]{2,1,0:T(8,128)(2,1)}, u32[]{:S(2)}, u32[]{:S(2)}) async-start(bf16[4,128,896]{2,1,0:T(8,128)(2,1)} %bitcast.22), calls=%async_computation.4 | async-start | bytes 1835008 | tf_op jit(solution)/shard_map/all_to_all | solution.py:162
  224.9 3.4 %pad_maximum_fusion.1 = bf16[2,1024,224]{2,0,1:T(2,128)(2,1)} fusion(bf16[1,1024,224]{2,0,1:T(2,128)(2,1)S(1)} %copy.47, bf16[1,1024,224]{2,0,1:T(2,128)(2,1)S(1)} %copy.46), kind=kLoop, calls=%fused_computation.47 | loop fusion | flops 1835008 | bytes 1835008 | tf_op jit(solution)/shard_map/stack | solution.py:71
  228.3 1.9 gather_fusion.1
  230.9 11.7 %all-to-all-done.3 = bf16[4,128,896]{2,1,0:T(8,128)(2,1)} async-done(((bf16[4,128,896]{2,1,0:T(8,128)(2,1)}), bf16[4,128,896]{2,1,0:T(8,128)(2,1)}, u32[]{:S(2)}, u32[]{:S(2)}) %all-to-all-start.3) | async-done | bytes 917536 | tf_op jit(solution)/shard_map/all_to_all | solution.py:162
  (78 shorter events, 24.9 us)
Async XLA Ops:
  7.2 5.3 %copy-start = (bf16[128,1792]{1,0:T(8,128)(2,1)S(1)}, bf16[128,1792]{1,0:T(8,128)(2,1)}, u32[]{:S(2)}) copy-start(bf16[128,1792]{1,0:T(8,128)(2,1)} %param.10) | copy-start | bytes 1376260
  7.2 5.5 %copy-start.5 = (f32[1792]{0:T(1024)S(1)}, f32[1792]{0:T(1024)}, u32[]{:S(2)}) copy-start(f32[1792]{0:T(1024)} %param.11) | copy-start | bytes 21508
  7.2 86.9 %all-gather.3.cloned.1.call-start = ((), (), s32[]{:S(2)}) async-start(), calls=%async_computation.5 | async-start | bytes 4257792 | tf_op jit(solution)/shard_map/all_gather | solution.py:77
  9.8 191.0 %all-gather.5.cloned.1.call-start = ((), (), s32[]{:S(2)}) async-start(), calls=%async_computation.6 | async-start | bytes 9934848 | tf_op jit(solution)/shard_map/all_gather | solution.py:77
  12.4 232.5 %reduce-scatter.2.cloned.1.call-start = ((), (), s32[]{:S(2)}) async-start(), calls=%async_computation.7 | async-start | bytes 1146880 | tf_op jit(solution)/shard_map/reduce_scatter | solution.py:161
  13.0 29.9 %copy-start.4 = (bf16[1,2,64,224]{3,2,1,0:T(8,128)(2,1)S(1)}, bf16[1,2,64,224]{3,2,1,0:T(8,128)(2,1)}, u32[]{:S(2)}) copy-start(bf16[1,2,64,224]{3,2,1,0:T(8,128)(2,1)} %param.18) | copy-start | bytes 172036
  13.0 31.7 %copy-start.7 = (f32[3,224]{1,0:T(4,128)S(1)}, f32[3,224]{1,0:T(4,128)}, u32[]{:S(2)}) copy-start(f32[3,224]{1,0:T(4,128)} %param.17) | copy-start | bytes 8068
  40.3 5.5 %collective-permute-start = (bf16[4,128,1792]{2,1,0:T(8,128)(2,1)S(1)}, bf16[4,128,1792]{2,1,0:T(8,128)(2,1)}, u32[]{:S(2)}, u32[]{:S(2)}) collective-permute-start(bf16[4,128,1792]{2,1,0:T(8,128)(2,1)S(1)} %all_to_all.20), channel_id=1, source_target_pairs={{0,1},{1,0},{2,3},{3,2},{4,5},{5,4},{6,7},{7,6},{8,9},{9,8},{10,11... | collective-permute-start | bytes 5505032 | tf_op jit(solution)/shard_map/ppermute | solution.py:87
  44.5 64.3 %copy-start.3 = (bf16[1,64,224]{2,1,0:T(8,128)(2,1)}, bf16[1,64,224]{2,1,0:T(8,128)(2,1)S(1)}, u32[]{:S(2)}) copy-start(bf16[1,64,224]{2,1,0:T(8,128)(2,1)S(1)} %copy.75) | copy-start | bytes 86020
  128.0 1.4 copy-start.2
  133.0 6.7 %collective-permute-start.1 = (bf16[512,1792]{1,0:T(8,128)(2,1)S(1)}, bf16[512,1792]{1,0:T(8,128)(2,1)S(1)}, u32[]{:S(2)}, u32[]{:S(2)}) collective-permute-start(bf16[512,1792]{1,0:T(8,128)(2,1)S(1)} %convolution_convert_fusion), channel_id=1, source_target_pairs={{0,1},{1,0},{2,3},{3,2},{4,5},{5,4},{6,7},{7,6},{8,9},{9,8},{10,11... | collective-permute-start | bytes 5505032 | tf_op jit(solution)/shard_map/ppermute | solution.py:87
  168.1 0.7 copy-start.6
  193.3 6.2 %collective-permute-start.2 = (bf16[512,1792]{1,0:T(8,128)(2,1)S(1)}, bf16[512,1792]{1,0:T(8,128)(2,1)}, u32[]{:S(2)}, u32[]{:S(2)}) collective-permute-start(bf16[512,1792]{1,0:T(8,128)(2,1)S(1)} %bitcast.70), channel_id=1, source_target_pairs={{0,1},{1,0},{2,3},{3,2},{4,5},{5,4},{6,7},{7,6},{8,9},{9,8},{10,11... | collective-permute-start | bytes 5505032 | tf_op jit(solution)/shard_map/ppermute | solution.py:87
  200.7 7.0 %copy-start.9 = (bf16[1792,2688]{1,0:T(8,128)(2,1)S(1)}, bf16[1792,2688]{1,0:T(8,128)(2,1)}, u32[]{:S(2)}) copy-start(bf16[1792,2688]{1,0:T(8,128)(2,1)} %all-gather.5.cloned.1.call-done) | copy-start | bytes 28901380
  210.1 4.7 %collective-permute-start.3 = (bf16[512,1792]{1,0:T(8,128)(2,1)S(1)}, bf16[512,1792]{1,0:T(8,128)(2,1)S(1)}, u32[]{:S(2)}, u32[]{:S(2)}) collective-permute-start(bf16[512,1792]{1,0:T(8,128)(2,1)S(1)} %convolution_convert_fusion.2), channel_id=1, source_target_pairs={{0,1},{1,0},{2,3},{3,2},{4,5},{5,4},{6,7},{7,6},{8,9},{9,8},{10,11... | collective-permute-start | bytes 5505032 | tf_op jit(solution)/shard_map/ppermute | solution.py:87
  218.5 4.7 %copy-start.8 = (s32[64]{0:T(128)S(1)}, s32[64]{0:T(128)}, u32[]{:S(2)}) copy-start(s32[64]{0:T(128)} %get-tuple-element.26) | copy-start | bytes 772
  218.6 5.5 %copy-start.1 = (bf16[1,1024,224]{1,2,0:T(8,128)(2,1)S(1)}, bf16[1,1024,224]{1,2,0:T(8,128)(2,1)}, u32[]{:S(2)}) copy-start(bf16[1,1024,224]{1,2,0:T(8,128)(2,1)} %get-tuple-element.10) | copy-start | bytes 1376260
  218.6 24.0 %all-to-all-start.3 = ((bf16[4,128,896]{2,1,0:T(8,128)(2,1)}), bf16[4,128,896]{2,1,0:T(8,128)(2,1)}, u32[]{:S(2)}, u32[]{:S(2)}) async-start(bf16[4,128,896]{2,1,0:T(8,128)(2,1)} %bitcast.22), calls=%async_computation.4 | async-start | bytes 1835008 | tf_op jit(solution)/shard_map/all_to_all | solution.py:162
Sparse Core Ops, SparseCore 0:
  11.2 82.8 all-gather.2
  96.7 103.9 all-gather.4
  218.7 26.1 reduce-scatter.1
where the time goes:
time: 254 us; the launch traced here: 253 us
  blocking collectives  78 us (31%)
  waiting for transfers between devices  66.3 us (26%)
  matrix products  37.2 us (15%)
  local copies, waits for them, and re-layouts  25.3 us (10%)
  other arithmetic  17.8 us (7%)
  between operations  14.8 us (6%)
  starting transfers between devices  13.9 us (5%)
    all_gather x2, waiting for transfers between devices, gather_packed(): lax.all_gather(jnp.concatenate(pieces, axis=1), 'req', axis=0, tiled=True)  45.7 us
    all_to_all x1, blocking collectives, local(): lax.all_to_all(jnp.tile(normed(tokens, norm_gain)[None], (nxt, 1, 1)), 't...  27.3 us
    all_to_all x1, blocking collectives, local(): lax.all_to_all(pair.reshape((nx, -1) + pair.shape[1:]), 'tpx', 0, 0, tile...  26.5 us
    all_to_all x1, blocking collectives, local(): lax.all_to_all(jnp.tile(normed(residual, ffn_gain)[None], (nx, 1, 1)), 't...  24.2 us
    all_to_all x1, waiting for transfers between devices, local(): lax.all_to_all(pair[:, cols:].reshape((nx, -1, cols)), 'tpx', 0, 0, tiled...  11.7 us
    dot_general x2, matrix products, mlp_rows(): gate_up = jnp.dot(rows, ffn_all, preferred_element_type=jnp.float32)  10.5 us
    ppermute x4, starting transfers between devices, core_swap(): return lax.ppermute(x, 'tpc', [(0, 1), (1, 0)])  9.13 us
    ppermute x4, waiting for transfers between devices, core_swap(): return lax.ppermute(x, 'tpc', [(0, 1), (1, 0)])  7.95 us
  transfers between devices with their start and end apart: 8, of which 7 were waited for; matrix products, arithmetic and copies ran while one was open for 25% of the time, Pallas kernels for 0%

commit v1 on v0

--- a/solution.py
+++ b/solution.py
@@ -74,7 +74,9 @@
 
 def gather_packed(pieces):
     widths = [p.shape[1] for p in pieces]
-    got = lax.all_gather(jnp.concatenate(pieces, axis=1), "req", axis=0, tiled=True)
+    value = jnp.concatenate(pieces, axis=1)
+    sent = jnp.stack([value] * lax.axis_size("req"))
+    got = jnp.concatenate(lax.all_to_all(sent, "req", 0, 0), axis=0)
     parts = []
     start = 0
     for w in widths:

time: 254 us -> 527 us (2.07)
  waiting for transfers between devices: 66.3 us -> 362 us
  blocking collectives: 78 us -> 25.7 us
  starting transfers between devices: 13.9 us -> 38.6 us
    all_to_all x0 -> x4, waiting for transfers between devices: none -> 340 us  [the longest x2 297 us: gather_packed(): got = jnp.concatenate(lax.all_to_all(sent, 'req', 0, 0), axis=0)]
    all_to_all x2 -> x0, blocking collectives: 51.5 us -> none  [the longest x1 27.3 us: local(): lax.all_to_all(jnp.tile(normed(tokens, norm_gain)[None], (nxt, 1, 1)), 't...]
    all_gather x2 -> x0, waiting for transfers between devices: 45.7 us -> none  [gather_packed(): lax.all_gather(jnp.concatenate(pieces, axis=1), 'req', axis=0, tiled=True)]
    all_to_all x0 -> x4, starting transfers between devices: none -> 26.1 us  [the longest x2 17.4 us: gather_packed(): got = jnp.concatenate(lax.all_to_all(sent, 'req', 0, 0), axis=0)]
    another operation x0 -> x2, local copies, waits for them, and re-layouts: none -> 6.57 us  [gather_packed(): sent = jnp.stack([value] * lax.axis_size('req'))]
  transfers between devices with their start and end apart: 8 -> 10, of which waited for: 7 -> 9; matrix products, arithmetic and copies ran while one was open for 25% -> 4% of each run, Pallas kernels for 0% -> 0%
where the time goes in v1:
time: 527 us; the launch traced here: 523 us
  waiting for transfers between devices  362 us (69%)
  matrix products  40.8 us (8%)
  starting transfers between devices  38.6 us (7%)
  local copies, waits for them, and re-layouts  26.3 us (5%)
  blocking collectives  25.7 us (5%)
  between operations  15.1 us (3%)
  other arithmetic  14.8 us (3%)
    all_to_all x2, waiting for transfers between devices, gather_packed(): got = jnp.concatenate(lax.all_to_all(sent, 'req', 0, 0), axis=0)  297 us
    all_to_all x1, blocking collectives, local(): lax.all_to_all(pair.reshape((nx, -1) + pair.shape[1:]), 'tpx', 0, 0, tile...  25.7 us
    all_to_all x1, waiting for transfers between devices, local(): lax.all_to_all(jnp.tile(normed(residual, ffn_gain)[None], (nx, 1, 1)), 't...  22.2 us
    all_to_all x1, waiting for transfers between devices, local(): lax.all_to_all(jnp.tile(normed(tokens, norm_gain)[None], (nxt, 1, 1)), 't...  21.4 us
    all_to_all x2, starting transfers between devices, gather_packed(): got = jnp.concatenate(lax.all_to_all(sent, 'req', 0, 0), axis=0)  17.4 us
    dot_general x2, matrix products, mlp_rows(): gate_up = jnp.dot(rows, ffn_all, preferred_element_type=jnp.float32)  13.2 us
    all_to_all x1, waiting for transfers between devices, local(): lax.all_to_all(pair[:, cols:].reshape((nx, -1, cols)), 'tpx', 0, 0, tiled...  11.1 us
  transfers between devices with their start and end apart: 10, of which 9 were waited for; matrix products, arithmetic and copies ran while one was open for 4% of the time, Pallas kernels for 0%

profile of v1, /device:TPU:1, one launch (start us, length us, event | category | flops | bytes accessed | tf_op | source)
XLA Modules:
  0.0 523.0 jit_solution(14560421678901557401)
XLA Ops:
  11.0 5.0 all-to-all-start
  16.1 21.4 %all-to-all-done = bf16[4,128,1792]{2,1,0:T(8,128)(2,1)S(1)} async-done(((bf16[4,128,1792]{2,1,0:T(8,128)(2,1)}), bf16[4,128,1792]{2,1,0:T(8,128)(2,1)S(1)}, u32[]{:S(2)}, u32[]{:S(2)}) %all-to-all-start) | async-done | bytes 1835040 | tf_op jit(solution)/shard_map/all_to_all | solution.py:119
  37.5 2.2 stack.15
  39.8 12.5 %all-to-all-start.1 = ((bf16[32,56,1120]{2,1,0:T(8,128)(2,1)}), bf16[32,56,1120]{2,1,0:T(8,128)(2,1)}, u32[]{:S(2)}, u32[]{:S(2)}) async-start(bf16[32,56,1120]{2,1,0:T(8,128)(2,1)} %stack.15), calls=%async_computation.1 | async-start | bytes 8257536 | tf_op jit(solution)/shard_map/all_to_all | solution.py:79
  52.3 2.2 collective-permute-start
  58.0 1.7 select_bitcast_fusion.1
  59.8 2.2 pad_maximum_fusion
  61.9 85.5 %all-to-all-done.1 = bf16[32,56,1120]{2,1,0:T(8,128)(2,1)} async-done(((bf16[32,56,1120]{2,1,0:T(8,128)(2,1)}), bf16[32,56,1120]{2,1,0:T(8,128)(2,1)}, u32[]{:S(2)}, u32[]{:S(2)}) %all-to-all-start.1) | async-done | bytes 4014112 | tf_op jit(solution)/shard_map/all_to_all | solution.py:79
  147.4 6.6 %fusion.13 = bf16[1024,896]{0,1:T(8,128)(2,1)S(1)} fusion(bf16[1024,1792]{1,0:T(8,128)(2,1)} %bitcast.70, bf16[1792,1120]{1,0:T(8,128)(2,1)} %bitcast.9), kind=kOutput, calls=%fused_computation.26 | convolution fusion | flops 3289251840 | bytes 8716288 | tf_op jit(solution)/shard_map/dot_general | solution.py:129
  157.1 1.9 reshape.307
  160.3 1.8 fusion.18
  164.1 5.7 %convolution_bitcast_fusion = f32[16,64,2,112]{3,1,2,0:T(8,128)S(1)} fusion(bf16[16,64,2,112]{1,3,2,0:T(8,128)(2,1)S(1)} %copy.33, bf16[16,64,2,112]{1,3,2,0:T(8,128)(2,1)S(1)} %copy.32, f32[16,2,64]{2,1,0:T(2,128)S(1)} %fusion.69, f32[16,2,64,128]{3,2,1,0:T(8,128)} %fusion.18), kind=kOutput, calls=%fused_computation.37 | convolution fusion | flops 61343872 | bytes 2891776 | tf_op jit(solution)/shard_map/bhqk,bkhd->bqhd/dot_general | solution.py:39
  173.2 1.9 convolution_convert_fusion
  175.1 1.6 collective-permute-start.1
  176.7 3.4 collective-permute-done.1
  180.2 1.9 add_convert_fusion.1
  182.0 25.7 %all_to_all.30 = bf16[4,128,1792]{2,1,0:T(8,128)(2,1)S(1)} all-to-all(bf16[4,128,1792]{2,1,0:T(8,128)(2,1)S(1)} %bitcast.69), channel_id=1, replica_groups=mesh['req'=32,'tpx'=4,'tpc'=2] {'tpx'}, dimensions={0} | all-to-all | bytes 3670016 | tf_op jit(solution)/shard_map/all_to_all | solution.py:149
  210.6 3.7 all-to-all-start.3
  214.4 22.2 %all-to-all-done.3 = bf16[4,128,1792]{2,1,0:T(8,128)(2,1)S(1)} async-done(((bf16[4,128,1792]{2,1,0:T(8,128)(2,1)}), bf16[4,128,1792]{2,1,0:T(8,128)(2,1)S(1)}, u32[]{:S(2)}, u32[]{:S(2)}) %all-to-all-start.3) | async-done | bytes 1835040 | tf_op jit(solution)/shard_map/all_to_all | solution.py:153
  236.6 4.3 stack.16
  241.0 5.0 all-to-all-start.4
  246.0 2.4 collective-permute-start.2
  248.4 3.5 collective-permute-done.2
  252.0 211.3 %all-to-all-done.4 = bf16[32,56,2688]{2,1,0:T(8,128)(2,1)} async-done(((bf16[32,56,2688]{2,1,0:T(8,128)(2,1)}), bf16[32,56,2688]{2,1,0:T(8,128)(2,1)}, u32[]{:S(2)}, u32[]{:S(2)}) %all-to-all-start.4) | async-done | bytes 9633824 | tf_op jit(solution)/shard_map/all_to_all | solution.py:79
  463.2 6.9 %fusion.1 = f32[512,1792]{1,0:T(8,128)S(1)} fusion(bf16[512,1792]{1,0:T(8,128)(2,1)} %collective-permute-done.2, bf16[1792,2688]{1,0:T(8,128)(2,1)} %bitcast.23), kind=kOutput, calls=%fused_computation.3 | convolution fusion | flops 3288334336 | bytes 11927552 | tf_op jit(solution)/shard_map/dot_general | solution.py:93
  470.1 4.2 convolution_convert_fusion.2
  475.9 6.3 %fusion.3 = f32[512,1792]{1,0:T(8,128)S(1)} fusion(bf16[512,1792]{1,0:T(8,128)(2,1)S(1)} %bitcast.73, bf16[1792,2688]{1,0:T(8,128)(2,1)} %bitcast.23), kind=kOutput, calls=%fused_computation.5 | convolution fusion | flops 3288334336 | bytes 11927552 | tf_op jit(solution)/shard_map/dot_general | solution.py:93
  482.2 4.3 add_convert_fusion
  487.9 4.6 all-to-all-start.5
  494.3 3.4 pad_maximum_fusion.1
  497.7 1.9 gather_fusion.1
  500.3 11.1 %all-to-all-done.5 = bf16[4,128,896]{2,1,0:T(8,128)(2,1)} async-done(((bf16[4,128,896]{2,1,0:T(8,128)(2,1)}), bf16[4,128,896]{2,1,0:T(8,128)(2,1)}, u32[]{:S(2)}, u32[]{:S(2)}) %all-to-all-start.5) | async-done | bytes 917536 | tf_op jit(solution)/shard_map/all_to_all | solution.py:164
  (78 shorter events, 29.4 us)
Async XLA Ops:
  11.0 5.0 copy-start.3
  11.0 5.1 copy-start.6
  11.0 26.6 %all-to-all-start = ((bf16[4,128,1792]{2,1,0:T(8,128)(2,1)}), bf16[4,128,1792]{2,1,0:T(8,128)(2,1)S(1)}, u32[]{:S(2)}, u32[]{:S(2)}) async-start(bf16[4,128,1792]{2,1,0:T(8,128)(2,1)} %tile.4), calls=%async_computation | async-start | bytes 3670016 | tf_op jit(solution)/shard_map/all_to_all | solution.py:119
  39.8 14.7 %copy-start.5 = (bf16[1,2,64,224]{3,2,1,0:T(8,128)(2,1)S(1)}, bf16[1,2,64,224]{3,2,1,0:T(8,128)(2,1)}, u32[]{:S(2)}) copy-start(bf16[1,2,64,224]{3,2,1,0:T(8,128)(2,1)} %param.18) | copy-start | bytes 172036
  39.8 16.5 %copy-start.8 = (f32[3,224]{1,0:T(4,128)S(1)}, f32[3,224]{1,0:T(4,128)}, u32[]{:S(2)}) copy-start(f32[3,224]{1,0:T(4,128)} %param.17) | copy-start | bytes 8068
  39.8 107.6 %all-to-all-start.1 = ((bf16[32,56,1120]{2,1,0:T(8,128)(2,1)}), bf16[32,56,1120]{2,1,0:T(8,128)(2,1)}, u32[]{:S(2)}, u32[]{:S(2)}) async-start(bf16[32,56,1120]{2,1,0:T(8,128)(2,1)} %stack.15), calls=%async_computation.1 | async-start | bytes 8257536 | tf_op jit(solution)/shard_map/all_to_all | solution.py:79
  52.3 5.8 %collective-permute-start = (bf16[4,128,1792]{2,1,0:T(8,128)(2,1)S(1)}, bf16[4,128,1792]{2,1,0:T(8,128)(2,1)}, u32[]{:S(2)}, u32[]{:S(2)}) collective-permute-start(bf16[4,128,1792]{2,1,0:T(8,128)(2,1)S(1)} %all-to-all-done), channel_id=1, source_target_pairs={{0,1},{1,0},{2,3},{3,2},{4,5},{5,4},{6,7},{7,6},{8,9},{9,8},{10,11... | collective-permute-start | bytes 5505032 | tf_op jit(solution)/shard_map/ppermute | solution.py:89
  175.1 5.1 collective-permute-start.1
  207.8 1.0 copy-start
  207.8 1.2 copy-start.7
  210.6 3.7 copy-start.2
  210.6 3.8 copy-start.4
  210.6 26.0 %all-to-all-start.3 = ((bf16[4,128,1792]{2,1,0:T(8,128)(2,1)}), bf16[4,128,1792]{2,1,0:T(8,128)(2,1)S(1)}, u32[]{:S(2)}, u32[]{:S(2)}) async-start(bf16[4,128,1792]{2,1,0:T(8,128)(2,1)} %tile.5), calls=%async_computation.3 | async-start | bytes 3670016 | tf_op jit(solution)/shard_map/all_to_all | solution.py:153
  241.0 222.3 %all-to-all-start.4 = ((bf16[32,56,2688]{2,1,0:T(8,128)(2,1)}), bf16[32,56,2688]{2,1,0:T(8,128)(2,1)}, u32[]{:S(2)}, u32[]{:S(2)}) async-start(bf16[32,56,2688]{2,1,0:T(8,128)(2,1)} %stack.16), calls=%async_computation.4 | async-start | bytes 19267584 | tf_op jit(solution)/shard_map/all_to_all | solution.py:79
  245.9 268.4 %reduce-scatter.2.cloned.1.call-start = ((), (), s32[]{:S(2)}) async-start(), calls=%async_computation.7 | async-start | bytes 1146880 | tf_op jit(solution)/shard_map/reduce_scatter | solution.py:163
  246.0 6.0 %collective-permute-start.2 = (bf16[512,1792]{1,0:T(8,128)(2,1)S(1)}, bf16[512,1792]{1,0:T(8,128)(2,1)}, u32[]{:S(2)}, u32[]{:S(2)}) collective-permute-start(bf16[512,1792]{1,0:T(8,128)(2,1)S(1)} %bitcast.72), channel_id=1, source_target_pairs={{0,1},{1,0},{2,3},{3,2},{4,5},{5,4},{6,7},{7,6},{8,9},{9,8},{10,11... | collective-permute-start | bytes 5505032 | tf_op jit(solution)/shard_map/ppermute | solution.py:89
  474.4 7.8 %collective-permute-start.3 = (bf16[512,1792]{1,0:T(8,128)(2,1)S(1)}, bf16[512,1792]{1,0:T(8,128)(2,1)S(1)}, u32[]{:S(2)}, u32[]{:S(2)}) collective-permute-start(bf16[512,1792]{1,0:T(8,128)(2,1)S(1)} %convolution_convert_fusion.2), channel_id=1, source_target_pairs={{0,1},{1,0},{2,3},{3,2},{4,5},{5,4},{6,7},{7,6},{8,9},{9,8},{10,11... | collective-permute-start | bytes 5505032 | tf_op jit(solution)/shard_map/ppermute | solution.py:89
  487.9 5.5 %copy-start.1 = (bf16[1,1024,224]{1,2,0:T(8,128)(2,1)S(1)}, bf16[1,1024,224]{1,2,0:T(8,128)(2,1)}, u32[]{:S(2)}) copy-start(bf16[1,1024,224]{1,2,0:T(8,128)(2,1)} %get-tuple-element.10) | copy-start | bytes 1376260
  487.9 23.4 %all-to-all-start.5 = ((bf16[4,128,896]{2,1,0:T(8,128)(2,1)}), bf16[4,128,896]{2,1,0:T(8,128)(2,1)}, u32[]{:S(2)}, u32[]{:S(2)}) async-start(bf16[4,128,896]{2,1,0:T(8,128)(2,1)} %bitcast.24), calls=%async_computation.6 | async-start | bytes 1835008 | tf_op jit(solution)/shard_map/all_to_all | solution.py:164
Sparse Core Ops, SparseCore 0:
  488.0 26.2 reduce-scatter.1
